TPU v7x, 256 devices: a whole 4x4x8 slice. The times are simulated.
256 devices in a mesh: tok: 32 (over x, z), hid: 8 (over y, core).
Axes of the slice: x: 4, y: 4, z: 8, core: 2. Of those that a mesh axis runs over, the one named last changes fastest.
Arguments:
- tokens: bfloat16 [16384, 5376], P('tok', 'hid'), may hold values from -6 to 6
- norm_gain: bfloat16 [1, 5376], P(None, 'hid'), may hold values from 0.099609375 to 1.8984375
- w_query: bfloat16 [5376, 4096], P('tok', 'hid'), may hold values from -2 to 2
- w_key: bfloat16 [5376, 2048], P('tok', 'hid'), may hold values from -1 to 1
- value_matrix: bfloat16 [5376, 2048], P('tok', 'hid'), may hold values from -0.078125 to 0.078125
- q_norm_gain: bfloat16 [1, 128], replicated, may hold values from 0.1 to 8
- k_norm_gain: bfloat16 [1, 128], replicated, may hold values from 0.1 to 8
- w_out: bfloat16 [4096, 5376], P('hid'), may hold values from -0.125 to 0.125
Outputs:
- attended: bfloat16 [16384, 5376], P('tok', 'hid')
All inputs are finite; a program needn't handle non-finite values.
Results may differ from a plain program's by a relative error of at most 0.017.
Values may be sent and summed in bfloat16 or wider, within the bound.
No kernel may reach another device: no remote copies, remote signals or barrier semaphores. Data moves between devices by JAX's collectives and lax.ppermute only.
A program may use at most 64 MiB of HBM per device.

v0:
```python
import math
import jax
import jax.numpy as jnp
from jax import lax
from jax.sharding import PartitionSpec as P

HEAD_SIZE = 128
WINDOW = 1024
score_scale = 168.0 ** (-0.5)


def shifted(value, axis, steps):
    count = lax.axis_size(axis)
    leading, last = (max(0, -steps), min(count, count - steps))
    return lax.ppermute(value, axis, [(source, source + steps) for source in range(leading, last)])


def head_norm(field, gain):
    count = field.shape[0]
    heads = field.reshape(count, -1, HEAD_SIZE)
    mean_square = jnp.mean(heads * heads, axis=-1, keepdims=True)
    scaled = (
        heads * lax.rsqrt(mean_square + 1e-06) * gain.astype(jnp.float32).reshape(1, 1, HEAD_SIZE)
    )
    return scaled.reshape(count, -1)


def rotate(field, positions):
    count = field.shape[0]
    heads = field.reshape(count, -1, HEAD_SIZE)
    half = HEAD_SIZE // 2
    inverse = jnp.exp(-math.log(10000.0) * jnp.arange(half, dtype=jnp.float32) * 2.0 / HEAD_SIZE)
    angles = positions.astype(jnp.float32)[:, None] * inverse[None, :]
    cosine = jnp.cos(angles)[:, None, :]
    sine = jnp.sin(angles)[:, None, :]
    first = heads[..., :half]
    second = heads[..., half:]
    turned = jnp.concatenate(
        [first * cosine - second * sine, second * cosine + first * sine], axis=-1
    )
    return turned.reshape(count, -1)


def local(tokens, norm_gain, w_query, w_key, value_matrix, q_norm_gain, k_norm_gain, w_out):
    rows = tokens.shape[0]
    gathered, gain_row = (
        lax.all_gather(tokens, "hid", axis=1, tiled=True),
        lax.all_gather(norm_gain, "hid", axis=1, tiled=True),
    )
    values32 = gathered.astype(jnp.float32)
    scale_rows = lax.rsqrt(jnp.mean(values32 * values32, axis=1, keepdims=True) + 1e-06)
    normed = (values32 * scale_rows * gain_row.astype(jnp.float32)).astype(jnp.bfloat16)
    width_query = w_query.shape[1]
    width_kv = w_key.shape[1]
    pieces = (
        lax.all_gather(w_query, "tok", axis=0, tiled=True),
        lax.all_gather(w_key, "tok", axis=0, tiled=True),
        lax.all_gather(value_matrix, "tok", axis=0, tiled=True),
    )
    query_raw, key_raw, value_raw = tuple(
        (jnp.dot(normed, piece, preferred_element_type=jnp.float32) for piece in pieces)
    )
    tok_index = lax.axis_index("tok")
    positions = tok_index * rows + jnp.arange(rows, dtype=jnp.int32)
    query = rotate(head_norm(query_raw, q_norm_gain), positions).astype(jnp.bfloat16)
    key = rotate(head_norm(key_raw, k_norm_gain), positions).astype(jnp.bfloat16)
    value_rows = value_raw.astype(jnp.bfloat16)
    joined = jnp.concatenate([key, value_rows], axis=1)
    reach = (WINDOW - 1 + rows - 1) // rows
    earlier = []
    moving = joined
    for offset in range(reach):
        moving = shifted(moving, "tok", 1)
        earlier = [moving] + earlier
    window_kv = jnp.concatenate(earlier + [joined], axis=0)
    window_extent = window_kv.shape[0]
    key_pos = (tok_index - reach) * rows + jnp.arange(window_extent, dtype=jnp.int32)
    kv_heads = width_kv // HEAD_SIZE
    query_group_count = width_query // HEAD_SIZE // kv_heads
    query_four_axes = query.reshape(rows, kv_heads, query_group_count, HEAD_SIZE)
    keys_three_axes = window_kv[:, :width_kv].reshape(window_extent, kv_heads, HEAD_SIZE)
    values_three_axes = window_kv[:, width_kv:].reshape(window_extent, kv_heads, HEAD_SIZE)
    scores = (
        jnp.einsum(
            "tkgd,skd->kgts", query_four_axes, keys_three_axes, preferred_element_type=jnp.float32
        )
        * score_scale
    )
    allowed = (
        (key_pos[None, :] <= positions[:, None])
        & (key_pos[None, :] > positions[:, None] - WINDOW)
        & (key_pos[None, :] >= 0)
    )
    masked = jnp.where(allowed, scores, -1e30)
    top = jnp.max(masked, axis=-1, keepdims=True)
    weights = jnp.where(allowed, jnp.exp(masked - top), 0.0)
    total = jnp.sum(weights, axis=-1)
    probs = weights.astype(jnp.bfloat16)
    mixed = jnp.einsum(
        "kgts,skd->tkgd", probs, values_three_axes, preferred_element_type=jnp.float32
    )
    mixed = mixed / jnp.transpose(total, (2, 0, 1))[..., None]
    heads_out = mixed.reshape(rows, width_query).astype(jnp.bfloat16)
    partial_value = jnp.dot(heads_out, w_out, preferred_element_type=jnp.float32)
    return lax.psum_scatter(
        partial_value.astype(jnp.bfloat16), "hid", scatter_dimension=1, tiled=True
    )


def solution(mesh):
    in_specs = (
        P("tok", "hid"),
        P(None, "hid"),
        P("tok", "hid"),
        P("tok", "hid"),
        P("tok", "hid"),
        P(),
        P(),
        P("hid", None),
    )
    out_specs = P("tok", "hid")
    return jax.shard_map(local, mesh=mesh, in_specs=in_specs, out_specs=out_specs, check_vma=False)
```

profile of v0, /device:TPU:2, one launch (start us, length us, event | category | flops | bytes accessed | tf_op | source)
XLA Modules:
  0.0 373.7 jit_solution(16431467091909844304)
XLA Ops:
  6.5 0.0 all-gather.5.cloned.1.call-start
  6.5 0.7 all-gather.5.cloned.1.call-update
  7.3 0.0 all-gather.7.cloned.1.call-start
  7.3 0.7 all-gather.7.cloned.1.call-update
  8.0 0.0 all-gather.9.cloned.1.call-start
  8.1 0.7 all-gather.9.cloned.1.call-update
  8.7 0.0 all-gather.11.cloned.1.call-start
  8.8 0.5 all-gather.11.cloned.1.call-update
  9.3 0.0 reduce-scatter.2.cloned.1.call-start
  9.4 1.3 dynamic-slice
  11.3 0.7 reduce
  12.0 0.2 dynamic-update-slice
  12.3 27.5 %all-reduce = bf16[5376]{0:T(1024)(128)(2,1)S(1)} all-reduce(bf16[5376]{0:T(1024)(128)(2,1)S(1)} %dynamic-update-slice), channel_id=1, replica_groups=mesh['tok'=32,'hid'=8] {'hid'}, use_global_device_ids=true, to_apply=%add | all-reduce | flops 5376 | bytes 21504
  39.8 0.7 bitcast_convert_fusion.1
  40.5 0.7 bitcast_convert_fusion
  41.1 0.5 multiply_cosine_fusion
  41.7 10.7 %all-gather.5.cloned.1.call-done = bf16[512,5376]{0,1:T(8,128)(2,1)} async-done(((bf16[512,672]{0,1:T(8,128)(2,1)}), bf16[512,5376]{0,1:T(8,128)(2,1)}) %all-gather.5.cloned.1.call-update) | async-done | bytes 5505040 | tf_op jit(solution)/shard_map/all_gather | solution.py:47
  52.4 3.8 %fusion.1 = f32[512]{0:T(512)S(1)} fusion(bf16[512,5376]{0,1:T(8,128)(2,1)} %all-gather.5.cloned.1.call-done), kind=kLoop, calls=%fused_computation.5 | loop fusion | flops 8257024 | bytes 5507072 | tf_op jit(solution)/shard_map/reduce_sum | solution.py:51
  56.2 76.4 %all-gather.7.cloned.1.call-done = bf16[5376,256]{1,0:T(8,128)(2,1)} async-done(((bf16[168,256]{1,0:T(8,128)(2,1)}), bf16[5376,256]{1,0:T(8,128)(2,1)}) %all-gather.7.cloned.1.call-update) | async-done | bytes 2752528 | tf_op jit(solution)/shard_map/all_gather | solution.py:57
  132.6 5.4 %multiply_reduce_fusion.1 = (f32[512,2]{0,1:T(2,128)S(1)}, f32[512,256]{0,1:T(8,128)S(1)}) fusion(bf16[5376,256]{1,0:T(8,128)(2,1)} %all-gather.7.cloned.1.call-done, bf16[512,5376]{0,1:T(8,128)(2,1)} %all-gather.5.cloned.1.call-done, f32[5376]{0:T(1024)S(1)} %mul.219, f32[512]{0:T(512)S(1)} %add_rsqrt_fusion.2), kind=kOutput, calls=%fused_computation.29 | convolution fusion | flops 1420557312 | bytes 8809472 | tf_op jit(solution)/shard_map/dot_general | solution.py:61
  138.1 0.1 multiply_multiply_fusion.1
  138.2 0.1 subtract_convert_fusion.1
  138.3 72.7 %all-gather.9.cloned.1.call-done = bf16[5376,256]{1,0:T(8,128)(2,1)} async-done(((bf16[168,256]{1,0:T(8,128)(2,1)}), bf16[5376,256]{1,0:T(8,128)(2,1)}) %all-gather.9.cloned.1.call-update) | async-done | bytes 2752528 | tf_op jit(solution)/shard_map/all_gather | solution.py:58
  211.0 5.4 %convolution_convert_fusion.1 = bf16[512,256]{0,1:T(8,128)(2,1)S(1)} fusion(bf16[5376,256]{1,0:T(8,128)(2,1)} %all-gather.9.cloned.1.call-done, bf16[512,5376]{0,1:T(8,128)(2,1)} %all-gather.5.cloned.1.call-done, f32[5376]{0:T(1024)S(1)} %mul.219, f32[512]{0:T(512)S(1)} %add_rsqrt_fusion.2), kind=kOutput, calls=%fused_computation.21 | convolution fusion | flops 1420427264 | bytes 8543232 | tf_op jit(solution)/shard_map/dot_general | solution.py:61
  216.5 2.9 collective-permute-start
  219.4 1.1 and_and_fusion
  220.6 10.4 %collective-permute-done = bf16[512,512]{0,1:T(8,128)(2,1)S(1)} collective-permute-done((bf16[512,512]{0,1:T(8,128)(2,1)S(1)}, bf16[512,512]{0,1:T(8,128)(2,1)S(1)}, u32[]{:S(2)}, u32[]{:S(2)}) %collective-permute-start) | collective-permute-done | bytes 524320 | tf_op jit(solution)/shard_map/ppermute | solution.py:15
  231.0 2.1 collective-permute-start.1
  233.1 63.4 %all-gather.11.cloned.1.call-done = bf16[5376,512]{1,0:T(8,128)(2,1)} async-done(((bf16[168,512]{1,0:T(8,128)(2,1)}), bf16[5376,512]{1,0:T(8,128)(2,1)}) %all-gather.11.cloned.1.call-update) | async-done | bytes 5505040 | tf_op jit(solution)/shard_map/all_gather | solution.py:56
  296.5 7.6 %multiply_reduce_fusion = (f32[512,4]{0,1:T(4,128)S(1)}, f32[512,512]{0,1:T(8,128)S(1)}) fusion(bf16[5376,512]{1,0:T(8,128)(2,1)} %all-gather.11.cloned.1.call-done, bf16[512,5376]{0,1:T(8,128)(2,1)} %all-gather.5.cloned.1.call-done, f32[5376]{0:T(1024)S(1)} %mul.219, f32[512]{0:T(512)S(1)} %add_rsqrt_fusion.2), kind=kOutput, calls=%fused_computation.23 | convolution fusion | flops 2830104576 | bytes 12090368 | tf_op jit(solution)/shard_map/dot_general | solution.py:61
  304.1 0.2 multiply_multiply_fusion
  304.3 0.2 subtract_convert_fusion
  304.6 0.0 collective-permute-done.1
  304.6 0.1 maximum_maximum_fusion
  304.7 0.1 fusion.30
  304.8 8.5 %fusion.31 = (f32[2,2,512]{2,1,0:T(2,128)S(1)}, bf16[2,2,512,1536]{2,3,1,0:T(8,128)(2,1)}) fusion(pred[512,1536]{0,1:T(8,128)(4,1)S(1)} %and_and_fusion, bf16[1536,2,128,1]{0,2,3,1:T(8,128)(2,1)S(1)} %bitcast.59, bf16[512,2,2,128]{0,3,2,1:T(8,128)(2,1)S(1)} %bitcast.60), kind=kOutput, calls=%fused_computation.51 | convolution fusion | flops 824182272 | bytes 8396800 | tf_op jit(solution)/shard_map/sub | solution.py:96
  313.3 3.8 %fusion.18 = bf16[512,2,2,128]{0,3,2,1:T(8,128)(2,1)S(1)} fusion(bf16[1536,2,128,1]{0,2,3,1:T(8,128)(2,1)S(1)} %bitcast.58, bf16[2,2,512,1536]{2,3,1,0:T(8,128)(2,1)} %get-tuple-element.18, f32[512,2,2]{0,2,1:T(2,128)S(1)} %bitcast.62), kind=kOutput, calls=%fused_computation.20 | convolution fusion | flops 805830656 | bytes 7610368 | tf_op jit(solution)/shard_map/kgts,skd->tkgd/dot_general | solution.py:99
  317.1 8.6 %convolution_convert_fusion = bf16[512,5376]{0,1:T(8,128)(2,1)} fusion(bf16[512,512]{0,1:T(8,128)(2,1)S(1)} %bitcast.61, bf16[512,5376]{1,0:T(8,128)(2,1)} %param.15), kind=kOutput, calls=%fused_computation.9 | convolution fusion | flops 2821324800 | bytes 11534336 | tf_op jit(solution)/shard_map/dot_general | solution.py:104
  325.7 0.0 reduce-scatter.2.cloned.1.call-update
  325.7 41.5 %reduce-scatter.2.cloned.1.call-done = bf16[512,672]{0,1:T(8,128)(2,1)} async-done(((bf16[512,5376]{0,1:T(8,128)(2,1)}), bf16[512,672]{0,1:T(8,128)(2,1)}) %reduce-scatter.2.cloned.1.call-update) | async-done | bytes 688144 | tf_op jit(solution)/shard_map/reduce_scatter | solution.py:105
  (13 shorter events, 0.2 us)
Async XLA Ops:
  6.5 45.9 %all-gather.5.cloned.1.call-start = ((), (), s32[]{:S(2)}) async-start(), calls=%async_computation.1 | async-start | bytes 6193152 | tf_op jit(solution)/shard_map/all_gather | solution.py:47
  7.3 125.3 %all-gather.7.cloned.1.call-start = ((), (), s32[]{:S(2)}) async-start(), calls=%async_computation.2 | async-start | bytes 2838528 | tf_op jit(solution)/shard_map/all_gather | solution.py:57
  8.0 203.0 %all-gather.9.cloned.1.call-start = ((), (), s32[]{:S(2)}) async-start(), calls=%async_computation.3 | async-start | bytes 2838528 | tf_op jit(solution)/shard_map/all_gather | solution.py:58
  8.7 287.8 %all-gather.11.cloned.1.call-start = ((), (), s32[]{:S(2)}) async-start(), calls=%async_computation.4 | async-start | bytes 5677056 | tf_op jit(solution)/shard_map/all_gather | solution.py:56
  9.3 357.9 %reduce-scatter.2.cloned.1.call-start = ((), (), s32[]{:S(2)}) async-start(), calls=%async_computation.5 | async-start | bytes 6193152 | tf_op jit(solution)/shard_map/reduce_scatter | solution.py:105
  216.5 14.5 %collective-permute-start = (bf16[512,512]{0,1:T(8,128)(2,1)S(1)}, bf16[512,512]{0,1:T(8,128)(2,1)S(1)}, u32[]{:S(2)}, u32[]{:S(2)}) collective-permute-start(bf16[512,512]{0,1:T(8,128)(2,1)S(1)} %pad_maximum_fusion), channel_id=1, source_target_pairs={{0,8},{8,16},{16,24},{24,32},{32,40},{40,48},{48,56},{56,64},{64,7... | collective-permute-start | bytes 1572872 | tf_op jit(solution)/shard_map/ppermute | solution.py:15
  231.0 73.5 %collective-permute-start.1 = (bf16[512,512]{0,1:T(8,128)(2,1)S(1)}, bf16[512,512]{0,1:T(8,128)(2,1)S(1)}, u32[]{:S(2)}, u32[]{:S(2)}) collective-permute-start(bf16[512,512]{0,1:T(8,128)(2,1)S(1)} %collective-permute-done), channel_id=1, source_target_pairs={{0,8},{8,16},{16,24},{24,32},{32,40},{40,48},{48,56},{56,64},{64,7... | collective-permute-start | bytes 1572872 | tf_op jit(solution)/shard_map/ppermute | solution.py:15
Sparse Core Ops, SparseCore 0:
  9.2 43.1 all-gather.4
  55.0 77.5 all-gather.6
  135.2 75.7 all-gather.8
  213.4 83.0 all-gather.10
  325.9 41.3 reduce-scatter.1
where the time goes:
time: 374 us
  waiting for transfers between devices  278 us (74%)
  matrix products  39.4 us (11%)
  blocking collectives  27.5 us (7%)
  between operations  14 us (4%)
  other arithmetic  8.29 us (2%)
  starting transfers between devices  5.17 us (1%)
    all_gather x1, waiting for transfers between devices, local(): lax.all_gather(w_key, 'tok', axis=0, tiled=True)  76.4 us
    all_gather x1, waiting for transfers between devices, local(): lax.all_gather(value_matrix, 'tok', axis=0, tiled=True)  72.7 us
    all_gather x1, waiting for transfers between devices, local(): lax.all_gather(w_query, 'tok', axis=0, tiled=True)  63.4 us
    reduce_scatter x1, waiting for transfers between devices, local(): lax.psum_scatter(partial_value.astype(jnp.bfloat16), 'hid', scatter_dimen...  41.5 us
    unnamed x1, blocking collectives  27.5 us
    dot_general x3, matrix products, local(): jnp.dot(normed, piece, preferred_element_type=jnp.float32)  18.5 us
    all_gather x1, waiting for transfers between devices, local(): lax.all_gather(tokens, 'hid', axis=1, tiled=True)  10.7 us
    ppermute x2, waiting for transfers between devices, shifted(): lax.ppermute(value, axis, [(source, source + steps) for source in range(l...  10.4 us
  transfers between devices with their start and end apart: 7, of which 6 were waited for; matrix products, arithmetic and copies ran while one was open for 8% of the time, Pallas kernels for 0%

commit v1 on v0

--- a/solution.py
+++ b/solution.py
@@ -52,9 +52,13 @@
     normed = (values32 * scale_rows * gain_row.astype(jnp.float32)).astype(jnp.bfloat16)
     width_query = w_query.shape[1]
     width_kv = w_key.shape[1]
+    turn_squares = lambda message, shard_axis: jnp.concatenate(
+        lax.all_to_all(jnp.stack(lax.axis_size(shard_axis) * [message], axis=0), shard_axis, 0, 0),
+        axis=0,
+    )
     pieces = (
         lax.all_gather(w_query, "tok", axis=0, tiled=True),
-        lax.all_gather(w_key, "tok", axis=0, tiled=True),
+        turn_squares(w_key, "tok"),
         lax.all_gather(value_matrix, "tok", axis=0, tiled=True),
     )
     query_raw, key_raw, value_raw = tuple(

time: 374 us -> 299 us (0.80)
  waiting for transfers between devices: 278 us -> 188 us
  starting transfers between devices: 5.17 us -> 16.8 us
  local copies, waits for them, and re-layouts: 1.62 us -> 6.79 us
    all_gather x1 -> x0, waiting for transfers between devices: 76.4 us -> none  [local(): lax.all_gather(w_key, 'tok', axis=0, tiled=True)]
    all_gather x1, waiting for transfers between devices: 72.7 us -> 37 us  [local(): lax.all_gather(value_matrix, 'tok', axis=0, tiled=True)]
    all_to_all x0 -> x1, waiting for transfers between devices: none -> 33.7 us  [local(): lax.all_to_all(jnp.stack(lax.axis_size(shard_axis) * [message], axis=0),...]
    all_to_all x0 -> x1, starting transfers between devices: none -> 11.6 us  [local(): lax.all_to_all(jnp.stack(lax.axis_size(shard_axis) * [message], axis=0),...]
    all_gather x1, waiting for transfers between devices: 10.7 us -> 0.01 us  [local(): lax.all_gather(tokens, 'hid', axis=1, tiled=True)]
  transfers between devices with their start and end apart: 7 -> 7, of which waited for: 6 -> 5; matrix products, arithmetic and copies ran while one was open for 8% -> 10% of each run, Pallas kernels for 0% -> 0%
where the time goes in v1:
time: 299 us
  waiting for transfers between devices  188 us (63%)
  matrix products  37.6 us (13%)
  blocking collectives  28.3 us (9%)
  starting transfers between devices  16.8 us (6%)
  between operations  14 us (5%)
  other arithmetic  7.49 us (3%)
  local copies, waits for them, and re-layouts  6.79 us (2%)
    all_gather x1, waiting for transfers between devices, local(): lax.all_gather(w_query, 'tok', axis=0, tiled=True)  63.4 us
    reduce_scatter x1, waiting for transfers between devices, local(): lax.psum_scatter(partial_value.astype(jnp.bfloat16), 'hid', scatter_dimen...  41.4 us
    all_gather x1, waiting for transfers between devices, local(): lax.all_gather(value_matrix, 'tok', axis=0, tiled=True)  37 us
    all_to_all x1, waiting for transfers between devices, local(): lax.all_to_all(jnp.stack(lax.axis_size(shard_axis) * [message], axis=0),...  33.7 us
    unnamed x1, blocking collectives  28.3 us
    dot_general x3, matrix products, local(): jnp.dot(normed, piece, preferred_element_type=jnp.float32)  16.7 us
    all_to_all x1, starting transfers between devices, local(): lax.all_to_all(jnp.stack(lax.axis_size(shard_axis) * [message], axis=0),...  11.6 us
    ppermute x2, waiting for transfers between devices, shifted(): lax.ppermute(value, axis, [(source, source + steps) for source in range(l...  10.4 us
  transfers between devices with their start and end apart: 7, of which 5 were waited for; matrix products, arithmetic and copies ran while one was open for 10% of the time, Pallas kernels for 0%

profile of v1, /device:TPU:2, one launch (start us, length us, event | category | flops | bytes accessed | tf_op | source)
XLA Modules:
  0.0 299.0 jit_solution(5108339447238413619)
XLA Ops:
  6.5 0.0 copy-start.4
  6.5 0.0 copy-start.1
  6.5 0.0 copy-start.2
  6.5 0.0 copy-start.3
  6.5 0.0 all-gather.4.cloned.1.call-start
  6.6 0.7 all-gather.4.cloned.1.call-update
  7.3 0.0 all-gather.6.cloned.1.call-start
  7.3 0.7 all-gather.6.cloned.1.call-update
  8.0 0.0 all-gather.8.cloned.1.call-start
  8.1 0.7 all-gather.8.cloned.1.call-update
  8.8 2.6 stack.2
  11.3 11.6 %all-to-all-start = ((bf16[32,168,256]{2,1,0:T(8,128)(2,1)}), bf16[32,168,256]{2,1,0:T(8,128)(2,1)S(1)}, u32[]{:S(2)}, u32[]{:S(2)}) async-start(bf16[32,168,256]{2,1,0:T(8,128)(2,1)} %stack.2), calls=%async_computation | async-start | bytes 5505024 | tf_op jit(solution)/shard_map/all_to_all | solution.py:56
  23.0 0.0 reduce-scatter.2.cloned.1.call-start
  23.0 0.0 copy-done.4
  23.0 0.6 dynamic-slice
  24.3 0.0 copy-done.1
  24.3 0.2 dynamic-update-slice
  24.6 28.3 %all-reduce = bf16[5376]{0:T(1024)(128)(2,1)S(1)} all-reduce(bf16[5376]{0:T(1024)(128)(2,1)S(1)} %dynamic-update-slice), channel_id=1, replica_groups=mesh['tok'=32,'hid'=8] {'hid'}, use_global_device_ids=true, to_apply=%add | all-reduce | flops 5376 | bytes 21504
  52.9 0.0 copy-done.2
  52.9 0.0 copy-done.3
  52.9 0.5 multiply_cosine_fusion
  53.5 33.7 %all-to-all-done = bf16[32,168,256]{2,1,0:T(8,128)(2,1)S(1)} async-done(((bf16[32,168,256]{2,1,0:T(8,128)(2,1)}), bf16[32,168,256]{2,1,0:T(8,128)(2,1)S(1)}, u32[]{:S(2)}, u32[]{:S(2)}) %all-to-all-start) | async-done | bytes 2752544 | tf_op jit(solution)/shard_map/all_to_all | solution.py:56
  87.2 3.0 %copy.14 = bf16[256,5376]{1,0:T(8,128)(2,1)} copy(bf16[256,5376]{0,1:T(8,128)(2,1)S(1)} %bitcast.62) | data formatting | bytes 5505024 | tf_op jit(solution)/shard_map/dot_general | solution.py:65
  90.2 0.0 all-gather.4.cloned.1.call-done
  90.2 0.0 copy-start
  90.2 3.9 %fusion.1 = f32[512]{0:T(512)S(1)} fusion(bf16[512,5376]{0,1:T(8,128)(2,1)} %all-gather.4.cloned.1.call-done), kind=kLoop, calls=%fused_computation.5 | loop fusion | flops 8257024 | bytes 5507072 | tf_op jit(solution)/shard_map/reduce_sum | solution.py:51
  94.1 0.3 copy-done
  94.4 3.7 %multiply_reduce_fusion.1 = (f32[512,2]{0,1:T(2,128)S(1)}, f32[512,2,128]{0,2,1:T(8,128)S(1)}) fusion(bf16[2,128,5376]{2,1,0:T(8,128)(2,1)} %bitcast.63, f32[5376]{0:T(1024)S(1)} %mul.219, f32[512]{0:T(512)S(1)} %add_rsqrt_fusion.2, bf16[512,5376]{0,1:T(8,128)(2,1)S(1)} %copy-done), kind=kOutput, calls=%fused_computation.31 | convolution fusion | flops 1420557312 | bytes 8809472 | tf_op jit(solution)/shard_map/dot_general | solution.py:65
  98.1 0.1 multiply_multiply_fusion.1
  98.2 0.1 subtract_convert_fusion.1
  98.3 37.0 %all-gather.6.cloned.1.call-done = bf16[5376,256]{1,0:T(8,128)(2,1)} async-done(((bf16[168,256]{1,0:T(8,128)(2,1)}), bf16[5376,256]{1,0:T(8,128)(2,1)}) %all-gather.6.cloned.1.call-update) | async-done | bytes 2752528 | tf_op jit(solution)/shard_map/all_gather | solution.py:62
  135.3 5.4 %convolution_convert_fusion.1 = bf16[512,256]{0,1:T(8,128)(2,1)S(1)} fusion(bf16[5376,256]{1,0:T(8,128)(2,1)} %all-gather.6.cloned.1.call-done, bf16[512,5376]{0,1:T(8,128)(2,1)} %all-gather.4.cloned.1.call-done, f32[5376]{0:T(1024)S(1)} %mul.219, f32[512]{0:T(512)S(1)} %add_rsqrt_fusion.2), kind=kOutput, calls=%fused_computation.23 | convolution fusion | flops 1420427264 | bytes 8543232 | tf_op jit(solution)/shard_map/dot_general | solution.py:65
  140.8 2.9 collective-permute-start
  143.7 1.1 and_and_fusion
  144.9 10.4 %collective-permute-done = bf16[512,512]{0,1:T(8,128)(2,1)S(1)} collective-permute-done((bf16[512,512]{0,1:T(8,128)(2,1)S(1)}, bf16[512,512]{0,1:T(8,128)(2,1)S(1)}, u32[]{:S(2)}, u32[]{:S(2)}) %collective-permute-start) | collective-permute-done | bytes 524320 | tf_op jit(solution)/shard_map/ppermute | solution.py:15
  155.3 2.1 collective-permute-start.1
  157.4 63.4 %all-gather.8.cloned.1.call-done = bf16[5376,512]{1,0:T(8,128)(2,1)} async-done(((bf16[168,512]{1,0:T(8,128)(2,1)}), bf16[5376,512]{1,0:T(8,128)(2,1)}) %all-gather.8.cloned.1.call-update) | async-done | bytes 5505040 | tf_op jit(solution)/shard_map/all_gather | solution.py:60
  220.8 7.6 %multiply_reduce_fusion = (f32[512,4]{0,1:T(4,128)S(1)}, f32[512,512]{0,1:T(8,128)S(1)}) fusion(bf16[5376,512]{1,0:T(8,128)(2,1)} %all-gather.8.cloned.1.call-done, bf16[512,5376]{0,1:T(8,128)(2,1)} %all-gather.4.cloned.1.call-done, f32[5376]{0:T(1024)S(1)} %mul.219, f32[512]{0:T(512)S(1)} %add_rsqrt_fusion.2), kind=kOutput, calls=%fused_computation.25 | convolution fusion | flops 2830104576 | bytes 12090368 | tf_op jit(solution)/shard_map/dot_general | solution.py:65
  228.5 0.2 multiply_multiply_fusion
  228.7 0.2 subtract_convert_fusion
  228.9 0.0 collective-permute-done.1
  228.9 1.1 maximum_maximum_fusion
  230.0 0.1 fusion.31
  230.1 8.5 %fusion.32 = (f32[2,2,512]{2,1,0:T(2,128)S(1)}, bf16[2,2,512,1536]{2,3,1,0:T(8,128)(2,1)}) fusion(pred[512,1536]{0,1:T(8,128)(4,1)S(1)} %and_and_fusion, bf16[1536,2,128,1]{0,2,3,1:T(8,128)(2,1)S(1)} %bitcast.67, bf16[512,2,2,128]{0,3,2,1:T(8,128)(2,1)S(1)} %bitcast.68), kind=kOutput, calls=%fused_computation.52 | convolution fusion | flops 824182272 | bytes 8396800 | tf_op jit(solution)/shard_map/sub | solution.py:100
  238.7 3.8 %fusion.20 = bf16[512,2,2,128]{0,3,2,1:T(8,128)(2,1)S(1)} fusion(bf16[1536,2,128,1]{0,2,3,1:T(8,128)(2,1)S(1)} %bitcast.66, bf16[2,2,512,1536]{2,3,1,0:T(8,128)(2,1)} %get-tuple-element.18, f32[512,2,2]{0,2,1:T(2,128)S(1)} %bitcast.70), kind=kOutput, calls=%fused_computation.22 | convolution fusion | flops 805830656 | bytes 7610368 | tf_op jit(solution)/shard_map/kgts,skd->tkgd/dot_general | solution.py:103
  242.4 8.6 %convolution_convert_fusion = bf16[512,5376]{0,1:T(8,128)(2,1)} fusion(bf16[512,512]{0,1:T(8,128)(2,1)S(1)} %bitcast.69, bf16[512,5376]{1,0:T(8,128)(2,1)} %param.15), kind=kOutput, calls=%fused_computation.9 | convolution fusion | flops 2821324800 | bytes 11534336 | tf_op jit(solution)/shard_map/dot_general | solution.py:108
  251.1 0.0 reduce-scatter.2.cloned.1.call-update
  251.1 41.4 %reduce-scatter.2.cloned.1.call-done = bf16[512,672]{0,1:T(8,128)(2,1)} async-done(((bf16[512,5376]{0,1:T(8,128)(2,1)}), bf16[512,672]{0,1:T(8,128)(2,1)}) %reduce-scatter.2.cloned.1.call-update) | async-done | bytes 688144 | tf_op jit(solution)/shard_map/reduce_scatter | solution.py:109
  (16 shorter events, 0.2 us)
Async XLA Ops:
  6.5 16.5 %copy-start.4 = (u32[256]{0:T(256)S(1)}, u32[256]{0:T(256)}, u32[]{:S(2)}) copy-start(u32[256]{0:T(256)} %constant.48) | copy-start | bytes 3076
  6.5 17.7 %copy-start.1 = (bf16[1,672]{1,0:T(2,128)(2,1)S(1)}, bf16[1,672]{1,0:T(2,128)(2,1)}, u32[]{:S(2)}) copy-start(bf16[1,672]{1,0:T(2,128)(2,1)} %param.9) | copy-start | bytes 4036
  6.5 46.3 %copy-start.2 = (bf16[1,128]{1,0:T(2,128)(2,1)S(1)}, bf16[1,128]{1,0:T(2,128)(2,1)}, u32[]{:S(2)}) copy-start(bf16[1,128]{1,0:T(2,128)(2,1)} %param.14) | copy-start | bytes 772
  6.5 46.4 %copy-start.3 = (bf16[1,128]{1,0:T(2,128)(2,1)S(1)}, bf16[1,128]{1,0:T(2,128)(2,1)}, u32[]{:S(2)}) copy-start(bf16[1,128]{1,0:T(2,128)(2,1)} %param.13) | copy-start | bytes 772
  6.5 83.6 %all-gather.4.cloned.1.call-start = ((), (), s32[]{:S(2)}) async-start(), calls=%async_computation.2 | async-start | bytes 6193152 | tf_op jit(solution)/shard_map/all_gather | solution.py:47
  7.3 128.0 %all-gather.6.cloned.1.call-start = ((), (), s32[]{:S(2)}) async-start(), calls=%async_computation.3 | async-start | bytes 2838528 | tf_op jit(solution)/shard_map/all_gather | solution.py:62
  8.0 212.8 %all-gather.8.cloned.1.call-start = ((), (), s32[]{:S(2)}) async-start(), calls=%async_computation.4 | async-start | bytes 5677056 | tf_op jit(solution)/shard_map/all_gather | solution.py:60
  11.3 75.8 %all-to-all-start = ((bf16[32,168,256]{2,1,0:T(8,128)(2,1)}), bf16[32,168,256]{2,1,0:T(8,128)(2,1)S(1)}, u32[]{:S(2)}, u32[]{:S(2)}) async-start(bf16[32,168,256]{2,1,0:T(8,128)(2,1)} %stack.2), calls=%async_computation | async-start | bytes 5505024 | tf_op jit(solution)/shard_map/all_to_all | solution.py:56
  23.0 269.5 %reduce-scatter.2.cloned.1.call-start = ((), (), s32[]{:S(2)}) async-start(), calls=%async_computation.5 | async-start | bytes 6193152 | tf_op jit(solution)/shard_map/reduce_scatter | solution.py:109
  90.2 4.2 %copy-start = (bf16[512,5376]{0,1:T(8,128)(2,1)S(1)}, bf16[512,5376]{0,1:T(8,128)(2,1)}, u32[]{:S(2)}) copy-start(bf16[512,5376]{0,1:T(8,128)(2,1)} %all-gather.4.cloned.1.call-done) | copy-start | bytes 16515076
  140.8 14.5 %collective-permute-start = (bf16[512,512]{0,1:T(8,128)(2,1)S(1)}, bf16[512,512]{0,1:T(8,128)(2,1)S(1)}, u32[]{:S(2)}, u32[]{:S(2)}) collective-permute-start(bf16[512,512]{0,1:T(8,128)(2,1)S(1)} %pad_maximum_fusion), channel_id=1, source_target_pairs={{0,8},{8,16},{16,24},{24,32},{32,40},{40,48},{48,56},{56,64},{64,7... | collective-permute-start | bytes 1572872 | tf_op jit(solution)/shard_map/ppermute | solution.py:15
  155.3 73.6 %collective-permute-start.1 = (bf16[512,512]{0,1:T(8,128)(2,1)S(1)}, bf16[512,512]{0,1:T(8,128)(2,1)}, u32[]{:S(2)}, u32[]{:S(2)}) collective-permute-start(bf16[512,512]{0,1:T(8,128)(2,1)S(1)} %collective-permute-done), channel_id=1, source_target_pairs={{0,8},{8,16},{16,24},{24,32},{32,40},{40,48},{48,56},{56,64},{64,7... | collective-permute-start | bytes 1572872 | tf_op jit(solution)/shard_map/ppermute | solution.py:15
Sparse Core Ops, SparseCore 0:
  9.2 43.3 all-gather.3
  55.2 80.0 all-gather.5
  137.9 82.9 all-gather.7
  251.2 41.2 reduce-scatter.1
